TPU v7x, 512 devices: a whole 4x8x8 slice. The times are simulated.
512 devices in a mesh: area: 128 (over z, y, core), blk: 4 (over x).
Axes of the slice: x: 4, y: 8, z: 8, core: 2. Of those that a mesh axis runs over, the one named last changes fastest.
Arguments:
- activity: float32 [1024, 4, 64, 128], P('area', 'blk'), may hold values from -8 to 8
- ext_input: bfloat16 [1024, 4, 64, 128], P('area', 'blk'), may hold values from -5 to 5
- weights: bfloat16 [384, 4, 128, 512], P('area', 'blk'), may hold values from -0.25 to 0.25
- slot_dst: int32 [384], P('area'), may hold values from 0 to 7
- slot_src: int32 [384], P('area'), may hold values from 0 to 1023, as said below
- slot_count: int32 [128], P('area'), may hold values from 3 to 3, as said below
- hebb_mask: int32 [384], P('area'), may hold values 0 or 1
Outputs:
- final_activity: float32 [1024, 4, 64, 128], P('area', 'blk')
- plasticity: bfloat16 [384, 4, 128, 512], P('area', 'blk')
Inputs may be any that keep to these rules, and one draw needn't show every extreme that they name: Index i of area holds area i // 4; sources lie in areas listed for it by a connectome over the areas that always lists the area itself, the areas beside it on both sides (counted round) and the opposite one. Slots 0, 1 and 2 of index i of area have their source sub-blocks held by indices (i - 1) mod 128, (i + 1) mod 128 and (i + 64) mod 128. Among the occupied slots of one index of area, at most 1 have source sub-blocks held by one index of area (slot_src // 8); some index of area reaches 1. `slot_count`: some index of area has all 3 slots occupied.
All inputs are finite; a program needn't handle non-finite values. No bound on the sum of `hebb_mask` on one device may be relied on, other than what follows from the above.
Results may differ from a plain program's by a relative error of at most 0.014.
Values may be sent and summed in bfloat16 or wider, within the bound.
No kernel may reach another device: no remote copies, remote signals or barrier semaphores. Data moves between devices by JAX's collectives and lax.ppermute only.
A program may use at most 64 MiB of HBM per device.

v0:
```python
import jax
import jax.numpy as jnp
from jax import lax
from jax.sharding import PartitionSpec as P

STEPS = 4
euler_step = 0.5


def centre(x):
    xf = x.astype(jnp.float32)
    return (xf - jnp.mean(xf, axis=-2, keepdims=True)).astype(jnp.bfloat16)


def body(activity, ext_input, weights, slot_dst, slot_src, slot_count, hebb_mask):
    n_areas = lax.axis_size("area")
    n_blk = lax.axis_size("blk")
    my_blk = lax.axis_index("blk")
    sub_dev = activity.shape[0]
    trials = activity.shape[2]
    quarter = activity.shape[3]
    slot_cap = slot_src.shape[0]
    sub_width = weights.shape[3]
    offsets = (-1, 1, n_areas // 2)
    occupied = jnp.arange(slot_cap) < slot_count[0]
    select = ((slot_dst[:, None] == jnp.arange(sub_dev)[None, :]) & occupied[:, None]).astype(
        jnp.float32
    )
    wanted = jnp.clip(slot_src % sub_dev, 0, sub_dev - 1).astype(jnp.int32)
    provide = []
    for k in range(slot_cap):
        perm = [(i, (i + offsets[k]) % n_areas) for i in range(n_areas)]
        provide.append(lax.ppermute(wanted[k], "area", perm))
    w_split = weights[:, 0].reshape(slot_cap, quarter, n_blk, quarter)
    w_parts = lax.all_to_all(w_split, "blk", split_axis=2, concat_axis=2, tiled=True)
    part_of_shift = (my_blk - jnp.arange(n_blk)) % n_blk
    w_shift = jnp.take(w_parts, part_of_shift, axis=2).transpose(0, 2, 1, 3)

    def n_of(area_idx, blk_idx):
        return area_idx * n_blk + blk_idx

    def exchange(rate_own):
        got = []
        for k in range(slot_cap):
            payload = lax.dynamic_index_in_dim(rate_own, provide[k], 0, keepdims=False)
            per_shift = []
            for s in range(n_blk):
                perm = [
                    (n_of(i, b), n_of((i - offsets[k]) % n_areas, (b + s) % n_blk))
                    for i in range(n_areas)
                    for b in range(n_blk)
                ]
                per_shift.append(lax.ppermute(payload, ("area", "blk"), perm))
            got.append(jnp.stack(per_shift))
        return jnp.stack(got)

    current = activity[:, 0]
    drive_in = ext_input[:, 0].astype(jnp.float32)
    rate_own = jnp.tanh(current).astype(jnp.bfloat16)
    pre_list = []
    post_list = []
    for step_idx in range(STEPS):
        presyn = exchange(rate_own)
        contrib = jnp.einsum("ksnq,ksqv->ksnv", presyn, w_shift, preferred_element_type=jnp.float32)
        partial_value = jnp.einsum(
            "kd,ksnv->sdnv", select, contrib, precision=lax.Precision.HIGHEST
        )
        summed = jnp.sum(partial_value.astype(jnp.bfloat16).astype(jnp.float32), axis=0)
        current = current + euler_step * (summed - current + drive_in)
        rate_own = jnp.tanh(current).astype(jnp.bfloat16)
        pre_list.append(presyn[:, 0])
        post_list.append(rate_own)
    final_state = current[:, None]
    pre_centered = centre(jnp.stack(pre_list, axis=1))
    post_centered = centre(jnp.stack(post_list, axis=0))
    post_sel = jnp.take(post_centered, slot_dst, axis=1).transpose(1, 0, 2, 3)
    post_whole = lax.all_gather(post_sel, "blk", axis=3, tiled=True)
    change = jnp.einsum(
        "ktnq,ktnu->kqu", pre_centered, post_whole, preferred_element_type=jnp.float32
    )
    gate_on = (occupied & (hebb_mask == 1)).astype(jnp.float32)
    norm_scale = (STEPS * trials) ** (-0.5)
    plasticity = (change * gate_on[:, None, None] * norm_scale).astype(jnp.bfloat16)[:, None]
    return (final_state, plasticity)


def solution(mesh):
    in_specs = (
        P("area", "blk", None, None),
        P("area", "blk", None, None),
        P("area", "blk", None, None),
        P("area"),
        P("area"),
        P("area"),
        P("area"),
    )
    out_specs = (P("area", "blk", None, None), P("area", "blk", None, None))
    return jax.shard_map(body, mesh=mesh, in_specs=in_specs, out_specs=out_specs, check_vma=False)
```

profile of v0, /device:TPU:2, one launch (start us, length us, event | category | flops | bytes accessed | tf_op | source)
XLA Modules:
  0.0 270.8 jit_solution(7294866537927108117)
XLA Ops:
  2.0 13.3 %collective-permute-start = (s32[]{:T(128)}, s32[]{:T(128)}, u32[]{:S(2)}, u32[]{:S(2)}) collective-permute-start(s32[]{:T(128)} %bitcast.2), channel_id=1, source_target_pairs={{0,508},{4,0},{8,4},{12,8},{16,12},{20,16},{24,20},{28,24},{32,28}... | collective-permute-start | bytes 20 | tf_op jit(solution)/shard_map/ppermute | solution.py:33
  21.3 5.0 %all-to-all-start = ((bf16[3,128,4,128]{3,1,0,2:T(8,128)(2,1)}), bf16[3,128,4,128]{3,1,0,2:T(8,128)(2,1)S(1)}, u32[]{:S(2)}, u32[]{:S(2)}) async-start(bf16[3,128,4,128]{3,1,0,2:T(8,128)(2,1)} %copy.71), calls=%async_computation | async-start | bytes 786432 | tf_op jit(solution)/shard_map/all_to_all | solution.py:35
  35.1 3.4 %collective-permute-start.3 = (bf16[64,128]{1,0:T(8,128)(2,1)S(1)}, bf16[64,128]{1,0:T(8,128)(2,1)S(1)}, u32[]{:S(2)}, u32[]{:S(2)}) collective-permute-start(bf16[64,128]{1,0:T(8,128)(2,1)S(1)} %get-tuple-element.28), channel_id=1, source_target_pairs={{0,6},{1,7},{2,4},{3,5},{4,10},{5,11},{6,8},{7,9},{8,14},{9,15},{1... | collective-permute-start | bytes 49160 | tf_op jit(solution)/shard_map/ppermute | solution.py:53
  38.5 4.2 %collective-permute-start.2 = (bf16[64,128]{1,0:T(8,128)(2,1)S(1)}, bf16[64,128]{1,0:T(8,128)(2,1)S(1)}, u32[]{:S(2)}, u32[]{:S(2)}) collective-permute-start(bf16[64,128]{1,0:T(8,128)(2,1)S(1)} %get-tuple-element.28), channel_id=1, source_target_pairs={{0,5},{1,6},{2,7},{3,4},{4,9},{5,10},{6,11},{7,8},{8,13},{9,14},{1... | collective-permute-start | bytes 49160 | tf_op jit(solution)/shard_map/ppermute | solution.py:53
  48.2 7.0 %collective-permute-start.13 = (bf16[64,128]{1,0:T(8,128)(2,1)S(1)}, bf16[64,128]{1,0:T(8,128)(2,1)S(1)}, u32[]{:S(2)}, u32[]{:S(2)}) collective-permute-start(bf16[64,128]{1,0:T(8,128)(2,1)S(1)} %get-tuple-element.29), channel_id=1, source_target_pairs={{0,258},{1,259},{2,256},{3,257},{4,262},{5,263},{6,260},{7,261},{8... | collective-permute-start | bytes 49160 | tf_op jit(solution)/shard_map/ppermute | solution.py:53
  55.2 6.4 %collective-permute-start.12 = (bf16[64,128]{1,0:T(8,128)(2,1)S(1)}, bf16[64,128]{1,0:T(8,128)(2,1)S(1)}, u32[]{:S(2)}, u32[]{:S(2)}) collective-permute-start(bf16[64,128]{1,0:T(8,128)(2,1)S(1)} %get-tuple-element.29), channel_id=1, source_target_pairs={{0,257},{1,258},{2,259},{3,256},{4,261},{5,262},{6,263},{7,260},{8... | collective-permute-start | bytes 49160 | tf_op jit(solution)/shard_map/ppermute | solution.py:53
  61.6 5.7 %collective-permute-start.11 = (bf16[64,128]{1,0:T(8,128)(2,1)S(1)}, bf16[64,128]{1,0:T(8,128)(2,1)S(1)}, u32[]{:S(2)}, u32[]{:S(2)}) collective-permute-start(bf16[64,128]{1,0:T(8,128)(2,1)S(1)} %get-tuple-element.29), channel_id=1, source_target_pairs={{0,256},{1,257},{2,258},{3,259},{4,260},{5,261},{6,262},{7,263},{8... | collective-permute-start | bytes 49160 | tf_op jit(solution)/shard_map/ppermute | solution.py:53
  67.3 3.8 %collective-permute-start.9 = (bf16[64,128]{1,0:T(8,128)(2,1)S(1)}, bf16[64,128]{1,0:T(8,128)(2,1)S(1)}, u32[]{:S(2)}, u32[]{:S(2)}) collective-permute-start(bf16[64,128]{1,0:T(8,128)(2,1)S(1)} %get-tuple-element.30), channel_id=1, source_target_pairs={{0,511},{1,508},{2,509},{3,510},{4,3},{5,0},{6,1},{7,2},{8,7},{9,4... | collective-permute-start | bytes 49160 | tf_op jit(solution)/shard_map/ppermute | solution.py:53
  71.1 5.5 %collective-permute-start.8 = (bf16[64,128]{1,0:T(8,128)(2,1)S(1)}, bf16[64,128]{1,0:T(8,128)(2,1)S(1)}, u32[]{:S(2)}, u32[]{:S(2)}) collective-permute-start(bf16[64,128]{1,0:T(8,128)(2,1)S(1)} %get-tuple-element.30), channel_id=1, source_target_pairs={{0,510},{1,511},{2,508},{3,509},{4,2},{5,3},{6,0},{7,1},{8,6},{9,7... | collective-permute-start | bytes 49160 | tf_op jit(solution)/shard_map/ppermute | solution.py:53
  76.6 4.9 %collective-permute-start.7 = (bf16[64,128]{1,0:T(8,128)(2,1)S(1)}, bf16[64,128]{1,0:T(8,128)(2,1)S(1)}, u32[]{:S(2)}, u32[]{:S(2)}) collective-permute-start(bf16[64,128]{1,0:T(8,128)(2,1)S(1)} %get-tuple-element.30), channel_id=1, source_target_pairs={{0,509},{1,510},{2,511},{3,508},{4,1},{5,2},{6,3},{7,0},{8,5},{9,6... | collective-permute-start | bytes 49160 | tf_op jit(solution)/shard_map/ppermute | solution.py:53
  81.5 3.4 %collective-permute-start.6 = (bf16[64,128]{1,0:T(8,128)(2,1)S(1)}, bf16[64,128]{1,0:T(8,128)(2,1)S(1)}, u32[]{:S(2)}, u32[]{:S(2)}) collective-permute-start(bf16[64,128]{1,0:T(8,128)(2,1)S(1)} %get-tuple-element.30), channel_id=1, source_target_pairs={{0,508},{1,509},{2,510},{3,511},{4,0},{5,1},{6,2},{7,3},{8,4},{9,5... | collective-permute-start | bytes 49160 | tf_op jit(solution)/shard_map/ppermute | solution.py:53
  97.5 8.4 %collective-permute-start.26 = (bf16[64,128]{1,0:T(8,128)(2,1)S(1)}, bf16[64,128]{1,0:T(8,128)(2,1)S(1)}, u32[]{:S(2)}, u32[]{:S(2)}) collective-permute-start(bf16[64,128]{1,0:T(8,128)(2,1)S(1)} %get-tuple-element.26), channel_id=1, source_target_pairs={{0,259},{1,256},{2,257},{3,258},{4,263},{5,260},{6,261},{7,262},{8... | collective-permute-start | bytes 49160 | tf_op jit(solution)/shard_map/ppermute | solution.py:53
  105.9 3.4 %collective-permute-start.25 = (bf16[64,128]{1,0:T(8,128)(2,1)S(1)}, bf16[64,128]{1,0:T(8,128)(2,1)S(1)}, u32[]{:S(2)}, u32[]{:S(2)}) collective-permute-start(bf16[64,128]{1,0:T(8,128)(2,1)S(1)} %get-tuple-element.26), channel_id=1, source_target_pairs={{0,258},{1,259},{2,256},{3,257},{4,262},{5,263},{6,260},{7,261},{8... | collective-permute-start | bytes 49160 | tf_op jit(solution)/shard_map/ppermute | solution.py:53
  109.4 9.0 %collective-permute-start.24 = (bf16[64,128]{1,0:T(8,128)(2,1)S(1)}, bf16[64,128]{1,0:T(8,128)(2,1)S(1)}, u32[]{:S(2)}, u32[]{:S(2)}) collective-permute-start(bf16[64,128]{1,0:T(8,128)(2,1)S(1)} %get-tuple-element.26), channel_id=1, source_target_pairs={{0,257},{1,258},{2,259},{3,256},{4,261},{5,262},{6,263},{7,260},{8... | collective-permute-start | bytes 49160 | tf_op jit(solution)/shard_map/ppermute | solution.py:53
  120.4 6.4 %collective-permute-start.22 = (bf16[64,128]{1,0:T(8,128)(2,1)S(1)}, bf16[64,128]{1,0:T(8,128)(2,1)S(1)}, u32[]{:S(2)}, u32[]{:S(2)}) collective-permute-start(bf16[64,128]{1,0:T(8,128)(2,1)S(1)} %get-tuple-element.27), channel_id=1, source_target_pairs={{0,511},{1,508},{2,509},{3,510},{4,3},{5,0},{6,1},{7,2},{8,7},{9,4... | collective-permute-start | bytes 49160 | tf_op jit(solution)/shard_map/ppermute | solution.py:53
  126.8 4.5 %collective-permute-start.21 = (bf16[64,128]{1,0:T(8,128)(2,1)S(1)}, bf16[64,128]{1,0:T(8,128)(2,1)S(1)}, u32[]{:S(2)}, u32[]{:S(2)}) collective-permute-start(bf16[64,128]{1,0:T(8,128)(2,1)S(1)} %get-tuple-element.27), channel_id=1, source_target_pairs={{0,510},{1,511},{2,508},{3,509},{4,2},{5,3},{6,0},{7,1},{8,6},{9,7... | collective-permute-start | bytes 49160 | tf_op jit(solution)/shard_map/ppermute | solution.py:53
  131.3 4.9 %collective-permute-start.20 = (bf16[64,128]{1,0:T(8,128)(2,1)S(1)}, bf16[64,128]{1,0:T(8,128)(2,1)S(1)}, u32[]{:S(2)}, u32[]{:S(2)}) collective-permute-start(bf16[64,128]{1,0:T(8,128)(2,1)S(1)} %get-tuple-element.27), channel_id=1, source_target_pairs={{0,509},{1,510},{2,511},{3,508},{4,1},{5,2},{6,3},{7,0},{8,5},{9,6... | collective-permute-start | bytes 49160 | tf_op jit(solution)/shard_map/ppermute | solution.py:53
  136.3 3.4 %collective-permute-start.19 = (bf16[64,128]{1,0:T(8,128)(2,1)S(1)}, bf16[64,128]{1,0:T(8,128)(2,1)S(1)}, u32[]{:S(2)}, u32[]{:S(2)}) collective-permute-start(bf16[64,128]{1,0:T(8,128)(2,1)S(1)} %get-tuple-element.27), channel_id=1, source_target_pairs={{0,508},{1,509},{2,510},{3,511},{4,0},{5,1},{6,2},{7,3},{8,4},{9,5... | collective-permute-start | bytes 49160 | tf_op jit(solution)/shard_map/ppermute | solution.py:53
  151.3 9.2 %collective-permute-start.38 = (bf16[64,128]{1,0:T(8,128)(2,1)S(1)}, bf16[64,128]{1,0:T(8,128)(2,1)S(1)}, u32[]{:S(2)}, u32[]{:S(2)}) collective-permute-start(bf16[64,128]{1,0:T(8,128)(2,1)S(1)} %get-tuple-element.23), channel_id=1, source_target_pairs={{0,259},{1,256},{2,257},{3,258},{4,263},{5,260},{6,261},{7,262},{8... | collective-permute-start | bytes 49160 | tf_op jit(solution)/shard_map/ppermute | solution.py:53
  163.5 8.5 %collective-permute-start.36 = (bf16[64,128]{1,0:T(8,128)(2,1)S(1)}, bf16[64,128]{1,0:T(8,128)(2,1)S(1)}, u32[]{:S(2)}, u32[]{:S(2)}) collective-permute-start(bf16[64,128]{1,0:T(8,128)(2,1)S(1)} %get-tuple-element.23), channel_id=1, source_target_pairs={{0,257},{1,258},{2,259},{3,256},{4,261},{5,262},{6,263},{7,260},{8... | collective-permute-start | bytes 49160 | tf_op jit(solution)/shard_map/ppermute | solution.py:53
  174.5 6.3 %collective-permute-start.34 = (bf16[64,128]{1,0:T(8,128)(2,1)S(1)}, bf16[64,128]{1,0:T(8,128)(2,1)S(1)}, u32[]{:S(2)}, u32[]{:S(2)}) collective-permute-start(bf16[64,128]{1,0:T(8,128)(2,1)S(1)} %get-tuple-element.24), channel_id=1, source_target_pairs={{0,511},{1,508},{2,509},{3,510},{4,3},{5,0},{6,1},{7,2},{8,7},{9,4... | collective-permute-start | bytes 49160 | tf_op jit(solution)/shard_map/ppermute | solution.py:53
  180.8 5.1 %collective-permute-start.33 = (bf16[64,128]{1,0:T(8,128)(2,1)S(1)}, bf16[64,128]{1,0:T(8,128)(2,1)S(1)}, u32[]{:S(2)}, u32[]{:S(2)}) collective-permute-start(bf16[64,128]{1,0:T(8,128)(2,1)S(1)} %get-tuple-element.24), channel_id=1, source_target_pairs={{0,510},{1,511},{2,508},{3,509},{4,2},{5,3},{6,0},{7,1},{8,6},{9,7... | collective-permute-start | bytes 49160 | tf_op jit(solution)/shard_map/ppermute | solution.py:53
  185.9 4.8 %collective-permute-start.32 = (bf16[64,128]{1,0:T(8,128)(2,1)S(1)}, bf16[64,128]{1,0:T(8,128)(2,1)S(1)}, u32[]{:S(2)}, u32[]{:S(2)}) collective-permute-start(bf16[64,128]{1,0:T(8,128)(2,1)S(1)} %get-tuple-element.24), channel_id=1, source_target_pairs={{0,509},{1,510},{2,511},{3,508},{4,1},{5,2},{6,3},{7,0},{8,5},{9,6... | collective-permute-start | bytes 49160 | tf_op jit(solution)/shard_map/ppermute | solution.py:53
  190.7 3.6 %collective-permute-start.31 = (bf16[64,128]{1,0:T(8,128)(2,1)S(1)}, bf16[64,128]{1,0:T(8,128)(2,1)S(1)}, u32[]{:S(2)}, u32[]{:S(2)}) collective-permute-start(bf16[64,128]{1,0:T(8,128)(2,1)S(1)} %get-tuple-element.24), channel_id=1, source_target_pairs={{0,508},{1,509},{2,510},{3,511},{4,0},{5,1},{6,2},{7,3},{8,4},{9,5... | collective-permute-start | bytes 49160 | tf_op jit(solution)/shard_map/ppermute | solution.py:53
  206.0 8.7 %collective-permute-start.50 = (bf16[64,128]{1,0:T(8,128)(2,1)S(1)}, bf16[64,128]{1,0:T(8,128)(2,1)S(1)}, u32[]{:S(2)}, u32[]{:S(2)}) collective-permute-start(bf16[64,128]{1,0:T(8,128)(2,1)S(1)} %get-tuple-element.20), channel_id=1, source_target_pairs={{0,259},{1,256},{2,257},{3,258},{4,263},{5,260},{6,261},{7,262},{8... | collective-permute-start | bytes 49160 | tf_op jit(solution)/shard_map/ppermute | solution.py:53
  214.7 3.4 %collective-permute-start.49 = (bf16[64,128]{1,0:T(8,128)(2,1)S(1)}, bf16[64,128]{1,0:T(8,128)(2,1)S(1)}, u32[]{:S(2)}, u32[]{:S(2)}) collective-permute-start(bf16[64,128]{1,0:T(8,128)(2,1)S(1)} %get-tuple-element.20), channel_id=1, source_target_pairs={{0,258},{1,259},{2,256},{3,257},{4,262},{5,263},{6,260},{7,261},{8... | collective-permute-start | bytes 49160 | tf_op jit(solution)/shard_map/ppermute | solution.py:53
  218.2 9.0 %collective-permute-start.48 = (bf16[64,128]{1,0:T(8,128)(2,1)S(1)}, bf16[64,128]{1,0:T(8,128)(2,1)S(1)}, u32[]{:S(2)}, u32[]{:S(2)}) collective-permute-start(bf16[64,128]{1,0:T(8,128)(2,1)S(1)} %get-tuple-element.20), channel_id=1, source_target_pairs={{0,257},{1,258},{2,259},{3,256},{4,261},{5,262},{6,263},{7,260},{8... | collective-permute-start | bytes 49160 | tf_op jit(solution)/shard_map/ppermute | solution.py:53
  229.2 6.4 %collective-permute-start.46 = (bf16[64,128]{1,0:T(8,128)(2,1)S(1)}, bf16[64,128]{1,0:T(8,128)(2,1)S(1)}, u32[]{:S(2)}, u32[]{:S(2)}) collective-permute-start(bf16[64,128]{1,0:T(8,128)(2,1)S(1)} %get-tuple-element.21), channel_id=1, source_target_pairs={{0,511},{1,508},{2,509},{3,510},{4,3},{5,0},{6,1},{7,2},{8,7},{9,4... | collective-permute-start | bytes 49160 | tf_op jit(solution)/shard_map/ppermute | solution.py:53
  235.6 4.5 %collective-permute-start.45 = (bf16[64,128]{1,0:T(8,128)(2,1)S(1)}, bf16[64,128]{1,0:T(8,128)(2,1)S(1)}, u32[]{:S(2)}, u32[]{:S(2)}) collective-permute-start(bf16[64,128]{1,0:T(8,128)(2,1)S(1)} %get-tuple-element.21), channel_id=1, source_target_pairs={{0,510},{1,511},{2,508},{3,509},{4,2},{5,3},{6,0},{7,1},{8,6},{9,7... | collective-permute-start | bytes 49160 | tf_op jit(solution)/shard_map/ppermute | solution.py:53
  240.1 4.9 %collective-permute-start.44 = (bf16[64,128]{1,0:T(8,128)(2,1)S(1)}, bf16[64,128]{1,0:T(8,128)(2,1)S(1)}, u32[]{:S(2)}, u32[]{:S(2)}) collective-permute-start(bf16[64,128]{1,0:T(8,128)(2,1)S(1)} %get-tuple-element.21), channel_id=1, source_target_pairs={{0,509},{1,510},{2,511},{3,508},{4,1},{5,2},{6,3},{7,0},{8,5},{9,6... | collective-permute-start | bytes 49160 | tf_op jit(solution)/shard_map/ppermute | solution.py:53
  245.0 3.4 %collective-permute-start.43 = (bf16[64,128]{1,0:T(8,128)(2,1)S(1)}, bf16[64,128]{1,0:T(8,128)(2,1)S(1)}, u32[]{:S(2)}, u32[]{:S(2)}) collective-permute-start(bf16[64,128]{1,0:T(8,128)(2,1)S(1)} %get-tuple-element.21), channel_id=1, source_target_pairs={{0,508},{1,509},{2,510},{3,511},{4,0},{5,1},{6,2},{7,3},{8,4},{9,5... | collective-permute-start | bytes 49160 | tf_op jit(solution)/shard_map/ppermute | solution.py:53
  253.1 16.6 %all_gather.3 = bf16[3,4,64,512]{3,2,1,0:T(8,128)(2,1)S(1)} all-gather(bf16[3,4,64,128]{3,2,1,0:T(8,128)(2,1)S(1)} %broadcast_select_fusion), channel_id=1, replica_groups=mesh['area'=128,'blk'=4] {'blk'}, dimensions={3}, use_global_device_ids=true | all-gather | bytes 983040 | tf_op jit(solution)/shard_map/all_gather | solution.py:77
  (134 shorter events, 66.0 us)
Async XLA Ops:
  2.0 25.8 %collective-permute-start = (s32[]{:T(128)}, s32[]{:T(128)}, u32[]{:S(2)}, u32[]{:S(2)}) collective-permute-start(s32[]{:T(128)} %bitcast.2), channel_id=1, source_target_pairs={{0,508},{4,0},{8,4},{12,8},{16,12},{20,16},{24,20},{28,24},{32,28}... | collective-permute-start | bytes 20 | tf_op jit(solution)/shard_map/ppermute | solution.py:33
  21.3 65.1 %all-to-all-start = ((bf16[3,128,4,128]{3,1,0,2:T(8,128)(2,1)}), bf16[3,128,4,128]{3,1,0,2:T(8,128)(2,1)S(1)}, u32[]{:S(2)}, u32[]{:S(2)}) async-start(bf16[3,128,4,128]{3,1,0,2:T(8,128)(2,1)} %copy.71), calls=%async_computation | async-start | bytes 786432 | tf_op jit(solution)/shard_map/all_to_all | solution.py:35
  35.1 20.1 %collective-permute-start.3 = (bf16[64,128]{1,0:T(8,128)(2,1)S(1)}, bf16[64,128]{1,0:T(8,128)(2,1)S(1)}, u32[]{:S(2)}, u32[]{:S(2)}) collective-permute-start(bf16[64,128]{1,0:T(8,128)(2,1)S(1)} %get-tuple-element.28), channel_id=1, source_target_pairs={{0,6},{1,7},{2,4},{3,5},{4,10},{5,11},{6,8},{7,9},{8,14},{9,15},{1... | collective-permute-start | bytes 49160 | tf_op jit(solution)/shard_map/ppermute | solution.py:53
  38.5 23.1 %collective-permute-start.2 = (bf16[64,128]{1,0:T(8,128)(2,1)S(1)}, bf16[64,128]{1,0:T(8,128)(2,1)S(1)}, u32[]{:S(2)}, u32[]{:S(2)}) collective-permute-start(bf16[64,128]{1,0:T(8,128)(2,1)S(1)} %get-tuple-element.28), channel_id=1, source_target_pairs={{0,5},{1,6},{2,7},{3,4},{4,9},{5,10},{6,11},{7,8},{8,13},{9,14},{1... | collective-permute-start | bytes 49160 | tf_op jit(solution)/shard_map/ppermute | solution.py:53
  42.7 24.5 %collective-permute-start.1 = (bf16[64,128]{1,0:T(8,128)(2,1)S(1)}, bf16[64,128]{1,0:T(8,128)(2,1)S(1)}, u32[]{:S(2)}, u32[]{:S(2)}) collective-permute-start(bf16[64,128]{1,0:T(8,128)(2,1)S(1)} %get-tuple-element.28), channel_id=1, source_target_pairs={{0,4},{1,5},{2,6},{3,7},{4,8},{5,9},{6,10},{7,11},{8,12},{9,13},{1... | collective-permute-start | bytes 49160 | tf_op jit(solution)/shard_map/ppermute | solution.py:53
  45.3 25.8 %collective-permute-start.14 = (bf16[64,128]{1,0:T(8,128)(2,1)S(1)}, bf16[64,128]{1,0:T(8,128)(2,1)S(1)}, u32[]{:S(2)}, u32[]{:S(2)}) collective-permute-start(bf16[64,128]{1,0:T(8,128)(2,1)S(1)} %get-tuple-element.29), channel_id=1, source_target_pairs={{0,259},{1,256},{2,257},{3,258},{4,263},{5,260},{6,261},{7,262},{8... | collective-permute-start | bytes 49160 | tf_op jit(solution)/shard_map/ppermute | solution.py:53
  48.2 28.4 %collective-permute-start.13 = (bf16[64,128]{1,0:T(8,128)(2,1)S(1)}, bf16[64,128]{1,0:T(8,128)(2,1)S(1)}, u32[]{:S(2)}, u32[]{:S(2)}) collective-permute-start(bf16[64,128]{1,0:T(8,128)(2,1)S(1)} %get-tuple-element.29), channel_id=1, source_target_pairs={{0,258},{1,259},{2,256},{3,257},{4,262},{5,263},{6,260},{7,261},{8... | collective-permute-start | bytes 49160 | tf_op jit(solution)/shard_map/ppermute | solution.py:53
  55.2 26.3 %collective-permute-start.12 = (bf16[64,128]{1,0:T(8,128)(2,1)S(1)}, bf16[64,128]{1,0:T(8,128)(2,1)S(1)}, u32[]{:S(2)}, u32[]{:S(2)}) collective-permute-start(bf16[64,128]{1,0:T(8,128)(2,1)S(1)} %get-tuple-element.29), channel_id=1, source_target_pairs={{0,257},{1,258},{2,259},{3,256},{4,261},{5,262},{6,263},{7,260},{8... | collective-permute-start | bytes 49160 | tf_op jit(solution)/shard_map/ppermute | solution.py:53
  61.6 23.4 %collective-permute-start.11 = (bf16[64,128]{1,0:T(8,128)(2,1)S(1)}, bf16[64,128]{1,0:T(8,128)(2,1)S(1)}, u32[]{:S(2)}, u32[]{:S(2)}) collective-permute-start(bf16[64,128]{1,0:T(8,128)(2,1)S(1)} %get-tuple-element.29), channel_id=1, source_target_pairs={{0,256},{1,257},{2,258},{3,259},{4,260},{5,261},{6,262},{7,263},{8... | collective-permute-start | bytes 49160 | tf_op jit(solution)/shard_map/ppermute | solution.py:53
  93.3 25.1 %collective-permute-start.16 = (bf16[64,128]{1,0:T(8,128)(2,1)S(1)}, bf16[64,128]{1,0:T(8,128)(2,1)S(1)}, u32[]{:S(2)}, u32[]{:S(2)}) collective-permute-start(bf16[64,128]{1,0:T(8,128)(2,1)S(1)} %get-tuple-element.25), channel_id=1, source_target_pairs={{0,5},{1,6},{2,7},{3,4},{4,9},{5,10},{6,11},{7,8},{8,13},{9,14},{1... | collective-permute-start | bytes 49160 | tf_op jit(solution)/shard_map/ppermute | solution.py:53
  95.6 24.8 %collective-permute-start.15 = (bf16[64,128]{1,0:T(8,128)(2,1)S(1)}, bf16[64,128]{1,0:T(8,128)(2,1)S(1)}, u32[]{:S(2)}, u32[]{:S(2)}) collective-permute-start(bf16[64,128]{1,0:T(8,128)(2,1)S(1)} %get-tuple-element.25), channel_id=1, source_target_pairs={{0,4},{1,5},{2,6},{3,7},{4,8},{5,9},{6,10},{7,11},{8,12},{9,13},{1... | collective-permute-start | bytes 49160 | tf_op jit(solution)/shard_map/ppermute | solution.py:53
  97.5 29.3 %collective-permute-start.26 = (bf16[64,128]{1,0:T(8,128)(2,1)S(1)}, bf16[64,128]{1,0:T(8,128)(2,1)S(1)}, u32[]{:S(2)}, u32[]{:S(2)}) collective-permute-start(bf16[64,128]{1,0:T(8,128)(2,1)S(1)} %get-tuple-element.26), channel_id=1, source_target_pairs={{0,259},{1,256},{2,257},{3,258},{4,263},{5,260},{6,261},{7,262},{8... | collective-permute-start | bytes 49160 | tf_op jit(solution)/shard_map/ppermute | solution.py:53
  105.9 25.4 %collective-permute-start.25 = (bf16[64,128]{1,0:T(8,128)(2,1)S(1)}, bf16[64,128]{1,0:T(8,128)(2,1)S(1)}, u32[]{:S(2)}, u32[]{:S(2)}) collective-permute-start(bf16[64,128]{1,0:T(8,128)(2,1)S(1)} %get-tuple-element.26), channel_id=1, source_target_pairs={{0,258},{1,259},{2,256},{3,257},{4,262},{5,263},{6,260},{7,261},{8... | collective-permute-start | bytes 49160 | tf_op jit(solution)/shard_map/ppermute | solution.py:53
  109.4 26.9 %collective-permute-start.24 = (bf16[64,128]{1,0:T(8,128)(2,1)S(1)}, bf16[64,128]{1,0:T(8,128)(2,1)S(1)}, u32[]{:S(2)}, u32[]{:S(2)}) collective-permute-start(bf16[64,128]{1,0:T(8,128)(2,1)S(1)} %get-tuple-element.26), channel_id=1, source_target_pairs={{0,257},{1,258},{2,259},{3,256},{4,261},{5,262},{6,263},{7,260},{8... | collective-permute-start | bytes 49160 | tf_op jit(solution)/shard_map/ppermute | solution.py:53
  118.4 21.2 %collective-permute-start.23 = (bf16[64,128]{1,0:T(8,128)(2,1)S(1)}, bf16[64,128]{1,0:T(8,128)(2,1)S(1)}, u32[]{:S(2)}, u32[]{:S(2)}) collective-permute-start(bf16[64,128]{1,0:T(8,128)(2,1)S(1)} %get-tuple-element.26), channel_id=1, source_target_pairs={{0,256},{1,257},{2,258},{3,259},{4,260},{5,261},{6,262},{7,263},{8... | collective-permute-start | bytes 49160 | tf_op jit(solution)/shard_map/ppermute | solution.py:53
  120.4 19.3 %collective-permute-start.22 = (bf16[64,128]{1,0:T(8,128)(2,1)S(1)}, bf16[64,128]{1,0:T(8,128)(2,1)S(1)}, u32[]{:S(2)}, u32[]{:S(2)}) collective-permute-start(bf16[64,128]{1,0:T(8,128)(2,1)S(1)} %get-tuple-element.27), channel_id=1, source_target_pairs={{0,511},{1,508},{2,509},{3,510},{4,3},{5,0},{6,1},{7,2},{8,7},{9,4... | collective-permute-start | bytes 49160 | tf_op jit(solution)/shard_map/ppermute | solution.py:53
  144.3 19.1 %collective-permute-start.29 = (bf16[64,128]{1,0:T(8,128)(2,1)S(1)}, bf16[64,128]{1,0:T(8,128)(2,1)S(1)}, u32[]{:S(2)}, u32[]{:S(2)}) collective-permute-start(bf16[64,128]{1,0:T(8,128)(2,1)S(1)} %get-tuple-element.22), channel_id=1, source_target_pairs={{0,6},{1,7},{2,4},{3,5},{4,10},{5,11},{6,8},{7,9},{8,14},{9,15},{1... | collective-permute-start | bytes 49160 | tf_op jit(solution)/shard_map/ppermute | solution.py:53
  147.4 24.6 %collective-permute-start.28 = (bf16[64,128]{1,0:T(8,128)(2,1)S(1)}, bf16[64,128]{1,0:T(8,128)(2,1)S(1)}, u32[]{:S(2)}, u32[]{:S(2)}) collective-permute-start(bf16[64,128]{1,0:T(8,128)(2,1)S(1)} %get-tuple-element.22), channel_id=1, source_target_pairs={{0,5},{1,6},{2,7},{3,4},{4,9},{5,10},{6,11},{7,8},{8,13},{9,14},{1... | collective-permute-start | bytes 49160 | tf_op jit(solution)/shard_map/ppermute | solution.py:53
  149.3 25.1 %collective-permute-start.27 = (bf16[64,128]{1,0:T(8,128)(2,1)S(1)}, bf16[64,128]{1,0:T(8,128)(2,1)S(1)}, u32[]{:S(2)}, u32[]{:S(2)}) collective-permute-start(bf16[64,128]{1,0:T(8,128)(2,1)S(1)} %get-tuple-element.22), channel_id=1, source_target_pairs={{0,4},{1,5},{2,6},{3,7},{4,8},{5,9},{6,10},{7,11},{8,12},{9,13},{1... | collective-permute-start | bytes 49160 | tf_op jit(solution)/shard_map/ppermute | solution.py:53
  151.3 29.5 %collective-permute-start.38 = (bf16[64,128]{1,0:T(8,128)(2,1)S(1)}, bf16[64,128]{1,0:T(8,128)(2,1)S(1)}, u32[]{:S(2)}, u32[]{:S(2)}) collective-permute-start(bf16[64,128]{1,0:T(8,128)(2,1)S(1)} %get-tuple-element.23), channel_id=1, source_target_pairs={{0,259},{1,256},{2,257},{3,258},{4,263},{5,260},{6,261},{7,262},{8... | collective-permute-start | bytes 49160 | tf_op jit(solution)/shard_map/ppermute | solution.py:53
  160.5 25.4 %collective-permute-start.37 = (bf16[64,128]{1,0:T(8,128)(2,1)S(1)}, bf16[64,128]{1,0:T(8,128)(2,1)S(1)}, u32[]{:S(2)}, u32[]{:S(2)}) collective-permute-start(bf16[64,128]{1,0:T(8,128)(2,1)S(1)} %get-tuple-element.23), channel_id=1, source_target_pairs={{0,258},{1,259},{2,256},{3,257},{4,262},{5,263},{6,260},{7,261},{8... | collective-permute-start | bytes 49160 | tf_op jit(solution)/shard_map/ppermute | solution.py:53
  163.5 27.2 %collective-permute-start.36 = (bf16[64,128]{1,0:T(8,128)(2,1)S(1)}, bf16[64,128]{1,0:T(8,128)(2,1)S(1)}, u32[]{:S(2)}, u32[]{:S(2)}) collective-permute-start(bf16[64,128]{1,0:T(8,128)(2,1)S(1)} %get-tuple-element.23), channel_id=1, source_target_pairs={{0,257},{1,258},{2,259},{3,256},{4,261},{5,262},{6,263},{7,260},{8... | collective-permute-start | bytes 49160 | tf_op jit(solution)/shard_map/ppermute | solution.py:53
  172.0 22.3 %collective-permute-start.35 = (bf16[64,128]{1,0:T(8,128)(2,1)S(1)}, bf16[64,128]{1,0:T(8,128)(2,1)S(1)}, u32[]{:S(2)}, u32[]{:S(2)}) collective-permute-start(bf16[64,128]{1,0:T(8,128)(2,1)S(1)} %get-tuple-element.23), channel_id=1, source_target_pairs={{0,256},{1,257},{2,258},{3,259},{4,260},{5,261},{6,262},{7,263},{8... | collective-permute-start | bytes 49160 | tf_op jit(solution)/shard_map/ppermute | solution.py:53
  174.5 19.8 %collective-permute-start.34 = (bf16[64,128]{1,0:T(8,128)(2,1)S(1)}, bf16[64,128]{1,0:T(8,128)(2,1)S(1)}, u32[]{:S(2)}, u32[]{:S(2)}) collective-permute-start(bf16[64,128]{1,0:T(8,128)(2,1)S(1)} %get-tuple-element.24), channel_id=1, source_target_pairs={{0,511},{1,508},{2,509},{3,510},{4,3},{5,0},{6,1},{7,2},{8,7},{9,4... | collective-permute-start | bytes 49160 | tf_op jit(solution)/shard_map/ppermute | solution.py:53
  199.0 19.2 %collective-permute-start.41 = (bf16[64,128]{1,0:T(8,128)(2,1)S(1)}, bf16[64,128]{1,0:T(8,128)(2,1)S(1)}, u32[]{:S(2)}, u32[]{:S(2)}) collective-permute-start(bf16[64,128]{1,0:T(8,128)(2,1)S(1)} %get-tuple-element.19), channel_id=1, source_target_pairs={{0,6},{1,7},{2,4},{3,5},{4,10},{5,11},{6,8},{7,9},{8,14},{9,15},{1... | collective-permute-start | bytes 49160 | tf_op jit(solution)/shard_map/ppermute | solution.py:53
  201.9 25.3 %collective-permute-start.40 = (bf16[64,128]{1,0:T(8,128)(2,1)S(1)}, bf16[64,128]{1,0:T(8,128)(2,1)S(1)}, u32[]{:S(2)}, u32[]{:S(2)}) collective-permute-start(bf16[64,128]{1,0:T(8,128)(2,1)S(1)} %get-tuple-element.19), channel_id=1, source_target_pairs={{0,5},{1,6},{2,7},{3,4},{4,9},{5,10},{6,11},{7,8},{8,13},{9,14},{1... | collective-permute-start | bytes 49160 | tf_op jit(solution)/shard_map/ppermute | solution.py:53
  203.9 25.3 %collective-permute-start.39 = (bf16[64,128]{1,0:T(8,128)(2,1)S(1)}, bf16[64,128]{1,0:T(8,128)(2,1)S(1)}, u32[]{:S(2)}, u32[]{:S(2)}) collective-permute-start(bf16[64,128]{1,0:T(8,128)(2,1)S(1)} %get-tuple-element.19), channel_id=1, source_target_pairs={{0,4},{1,5},{2,6},{3,7},{4,8},{5,9},{6,10},{7,11},{8,12},{9,13},{1... | collective-permute-start | bytes 49160 | tf_op jit(solution)/shard_map/ppermute | solution.py:53
  206.0 29.6 %collective-permute-start.50 = (bf16[64,128]{1,0:T(8,128)(2,1)S(1)}, bf16[64,128]{1,0:T(8,128)(2,1)S(1)}, u32[]{:S(2)}, u32[]{:S(2)}) collective-permute-start(bf16[64,128]{1,0:T(8,128)(2,1)S(1)} %get-tuple-element.20), channel_id=1, source_target_pairs={{0,259},{1,256},{2,257},{3,258},{4,263},{5,260},{6,261},{7,262},{8... | collective-permute-start | bytes 49160 | tf_op jit(solution)/shard_map/ppermute | solution.py:53
  214.7 25.4 %collective-permute-start.49 = (bf16[64,128]{1,0:T(8,128)(2,1)S(1)}, bf16[64,128]{1,0:T(8,128)(2,1)S(1)}, u32[]{:S(2)}, u32[]{:S(2)}) collective-permute-start(bf16[64,128]{1,0:T(8,128)(2,1)S(1)} %get-tuple-element.20), channel_id=1, source_target_pairs={{0,258},{1,259},{2,256},{3,257},{4,262},{5,263},{6,260},{7,261},{8... | collective-permute-start | bytes 49160 | tf_op jit(solution)/shard_map/ppermute | solution.py:53
  218.2 26.9 %collective-permute-start.48 = (bf16[64,128]{1,0:T(8,128)(2,1)S(1)}, bf16[64,128]{1,0:T(8,128)(2,1)S(1)}, u32[]{:S(2)}, u32[]{:S(2)}) collective-permute-start(bf16[64,128]{1,0:T(8,128)(2,1)S(1)} %get-tuple-element.20), channel_id=1, source_target_pairs={{0,257},{1,258},{2,259},{3,256},{4,261},{5,262},{6,263},{7,260},{8... | collective-permute-start | bytes 49160 | tf_op jit(solution)/shard_map/ppermute | solution.py:53
  227.2 21.2 %collective-permute-start.47 = (bf16[64,128]{1,0:T(8,128)(2,1)S(1)}, bf16[64,128]{1,0:T(8,128)(2,1)S(1)}, u32[]{:S(2)}, u32[]{:S(2)}) collective-permute-start(bf16[64,128]{1,0:T(8,128)(2,1)S(1)} %get-tuple-element.20), channel_id=1, source_target_pairs={{0,256},{1,257},{2,258},{3,259},{4,260},{5,261},{6,262},{7,263},{8... | collective-permute-start | bytes 49160 | tf_op jit(solution)/shard_map/ppermute | solution.py:53
  229.2 19.3 %collective-permute-start.46 = (bf16[64,128]{1,0:T(8,128)(2,1)S(1)}, bf16[64,128]{1,0:T(8,128)(2,1)S(1)}, u32[]{:S(2)}, u32[]{:S(2)}) collective-permute-start(bf16[64,128]{1,0:T(8,128)(2,1)S(1)} %get-tuple-element.21), channel_id=1, source_target_pairs={{0,511},{1,508},{2,509},{3,510},{4,3},{5,0},{6,1},{7,2},{8,7},{9,4... | collective-permute-start | bytes 49160 | tf_op jit(solution)/shard_map/ppermute | solution.py:53
  (24 other events, 255.4 us)
where the time goes:
time: 272 us; the launch traced here: 271 us
  starting transfers between devices  227 us (83%)
  blocking collectives  16.6 us (6%)
  between operations  7.84 us (3%)
  waiting for transfers between devices  5.56 us (2%)
  matrix products  5.43 us (2%)
  local copies, waits for them, and re-layouts  4.86 us (2%)
  other arithmetic  3.04 us (1%)
    ppermute x48, starting transfers between devices, exchange(): per_shift.append(lax.ppermute(payload, ('area', 'blk'), perm))  205 us
    ppermute x3, starting transfers between devices, body(): provide.append(lax.ppermute(wanted[k], 'area', perm))  17.1 us
    all_gather x1, blocking collectives, body(): post_whole = lax.all_gather(post_sel, 'blk', axis=3, tiled=True)  16.6 us
    ppermute x48, waiting for transfers between devices, exchange(): per_shift.append(lax.ppermute(payload, ('area', 'blk'), perm))  5.55 us
  transfers between devices with their start and end apart: 52, of which 4 were waited for; matrix products, arithmetic and copies ran while one was open for 1% of the time, Pallas kernels for 0%

commit v1 on v0

--- a/solution.py
+++ b/solution.py
@@ -5,6 +5,28 @@
 
 STEPS = 4
 euler_step = 0.5
+
+
+def in_order(pieces, dim):
+    shape = list(pieces.shape[1:])
+    shape[dim] *= pieces.shape[0]
+    return jnp.moveaxis(pieces, 0, dim).reshape(shape)
+
+
+def gather_around(array, axis, dim):
+    size = lax.axis_size(axis)
+    pairs = [(i, (i + 1) % size) for i in range(size)]
+    back = [(b, a) for a, b in pairs]
+    lower, upper = ([], [])
+    for turn in range(size - 1):
+        if turn % 2 == 0:
+            lower.append(lax.ppermute(lower[-1] if lower else array, axis, pairs))
+        else:
+            upper.append(lax.ppermute(upper[-1] if upper else array, axis, back))
+    pieces = jnp.stack([*lower[::-1], array, *upper])
+    shift = lax.axis_index(axis) - len(lower)
+    pieces = pieces[(jnp.arange(size) - shift) % size]
+    return in_order(pieces, dim)
 
 
 def centre(x):
@@ -74,7 +96,7 @@
     pre_centered = centre(jnp.stack(pre_list, axis=1))
     post_centered = centre(jnp.stack(post_list, axis=0))
     post_sel = jnp.take(post_centered, slot_dst, axis=1).transpose(1, 0, 2, 3)
-    post_whole = lax.all_gather(post_sel, "blk", axis=3, tiled=True)
+    post_whole = gather_around(post_sel, "blk", 3)
     change = jnp.einsum(
         "ktnq,ktnu->kqu", pre_centered, post_whole, preferred_element_type=jnp.float32
     )

time: 272 us -> 275 us (1.011)
  the two profiles are of different devices: /device:TPU:2 before, /device:TPU:1 now
where the time goes in v1:
time: 275 us; the launch traced here: 273 us
  starting transfers between devices  234 us (85%)
  waiting for transfers between devices  16 us (6%)
  between operations  8.26 us (3%)
  local copies, waits for them, and re-layouts  6.19 us (2%)
  matrix products  5.42 us (2%)
  other arithmetic  3.25 us (1%)
    ppermute x48, starting transfers between devices, exchange(): per_shift.append(lax.ppermute(payload, ('area', 'blk'), perm))  203 us
    ppermute x3, starting transfers between devices, body(): provide.append(lax.ppermute(wanted[k], 'area', perm))  17.4 us
    ppermute x48, waiting for transfers between devices, exchange(): per_shift.append(lax.ppermute(payload, ('area', 'blk'), perm))  8.66 us
    ppermute x2, waiting for transfers between devices, gather_around(): lower.append(lax.ppermute(lower[-1] if lower else array, axis, pairs))  7.28 us
    ppermute x2, starting transfers between devices, gather_around(): lower.append(lax.ppermute(lower[-1] if lower else array, axis, pairs))  7.17 us
  transfers between devices with their start and end apart: 55, of which 10 were waited for; matrix products, arithmetic and copies ran while one was open for 1% of the time, Pallas kernels for 0%

profile of v1, /device:TPU:1, one launch (start us, length us, event | category | flops | bytes accessed | tf_op | source)
XLA Modules:
  0.0 273.0 jit_solution(1511801244197740867)
XLA Ops:
  2.0 8.7 %collective-permute-start = (s32[]{:T(128)}, s32[]{:T(128)}, u32[]{:S(2)}, u32[]{:S(2)}) collective-permute-start(s32[]{:T(128)} %bitcast.2), channel_id=1, source_target_pairs={{0,508},{4,0},{8,4},{12,8},{16,12},{20,16},{24,20},{28,24},{32,28}... | collective-permute-start | bytes 20 | tf_op jit(solution)/shard_map/ppermute | solution.py:55
  10.7 5.3 %collective-permute-start.10 = (s32[]{:T(128)}, s32[]{:T(128)}, u32[]{:S(2)}, u32[]{:S(2)}) collective-permute-start(s32[]{:T(128)} %bitcast.16), channel_id=1, source_target_pairs={{0,256},{4,260},{8,264},{12,268},{16,272},{20,276},{24,280},{28,28... | collective-permute-start | bytes 20 | tf_op jit(solution)/shard_map/ppermute | solution.py:55
  16.0 3.4 %collective-permute-start.5 = (s32[]{:T(128)}, s32[]{:T(128)}, u32[]{:S(2)}, u32[]{:S(2)}) collective-permute-start(s32[]{:T(128)} %bitcast.9), channel_id=1, source_target_pairs={{0,4},{4,8},{8,12},{12,16},{16,20},{20,24},{24,28},{28,32},{32,36}... | collective-permute-start | bytes 20 | tf_op jit(solution)/shard_map/ppermute | solution.py:55
  21.5 4.1 %all-to-all-start = ((bf16[3,128,4,128]{3,1,0,2:T(8,128)(2,1)}), bf16[3,128,4,128]{3,1,0,2:T(8,128)(2,1)S(1)}, u32[]{:S(2)}, u32[]{:S(2)}) async-start(bf16[3,128,4,128]{3,1,0,2:T(8,128)(2,1)} %copy.74), calls=%async_computation | async-start | bytes 786432 | tf_op jit(solution)/shard_map/all_to_all | solution.py:57
  33.8 5.1 %collective-permute-start.4 = (bf16[64,128]{1,0:T(8,128)(2,1)S(1)}, bf16[64,128]{1,0:T(8,128)(2,1)S(1)}, u32[]{:S(2)}, u32[]{:S(2)}) collective-permute-start(bf16[64,128]{1,0:T(8,128)(2,1)S(1)} %get-tuple-element.28), channel_id=1, source_target_pairs={{0,7},{1,4},{2,5},{3,6},{4,11},{5,8},{6,9},{7,10},{8,15},{9,12},{1... | collective-permute-start | bytes 49160 | tf_op jit(solution)/shard_map/ppermute | solution.py:75
  38.8 3.3 %collective-permute-start.3 = (bf16[64,128]{1,0:T(8,128)(2,1)S(1)}, bf16[64,128]{1,0:T(8,128)(2,1)S(1)}, u32[]{:S(2)}, u32[]{:S(2)}) collective-permute-start(bf16[64,128]{1,0:T(8,128)(2,1)S(1)} %get-tuple-element.28), channel_id=1, source_target_pairs={{0,6},{1,7},{2,4},{3,5},{4,10},{5,11},{6,8},{7,9},{8,14},{9,15},{1... | collective-permute-start | bytes 49160 | tf_op jit(solution)/shard_map/ppermute | solution.py:75
  48.1 3.5 %collective-permute-start.14 = (bf16[64,128]{1,0:T(8,128)(2,1)S(1)}, bf16[64,128]{1,0:T(8,128)(2,1)S(1)}, u32[]{:S(2)}, u32[]{:S(2)}) collective-permute-start(bf16[64,128]{1,0:T(8,128)(2,1)S(1)} %get-tuple-element.29), channel_id=1, source_target_pairs={{0,259},{1,256},{2,257},{3,258},{4,263},{5,260},{6,261},{7,262},{8... | collective-permute-start | bytes 49160 | tf_op jit(solution)/shard_map/ppermute | solution.py:75
  51.6 8.5 %collective-permute-start.13 = (bf16[64,128]{1,0:T(8,128)(2,1)S(1)}, bf16[64,128]{1,0:T(8,128)(2,1)S(1)}, u32[]{:S(2)}, u32[]{:S(2)}) collective-permute-start(bf16[64,128]{1,0:T(8,128)(2,1)S(1)} %get-tuple-element.29), channel_id=1, source_target_pairs={{0,258},{1,259},{2,256},{3,257},{4,262},{5,263},{6,260},{7,261},{8... | collective-permute-start | bytes 49160 | tf_op jit(solution)/shard_map/ppermute | solution.py:75
  62.0 5.8 %collective-permute-start.11 = (bf16[64,128]{1,0:T(8,128)(2,1)S(1)}, bf16[64,128]{1,0:T(8,128)(2,1)S(1)}, u32[]{:S(2)}, u32[]{:S(2)}) collective-permute-start(bf16[64,128]{1,0:T(8,128)(2,1)S(1)} %get-tuple-element.29), channel_id=1, source_target_pairs={{0,256},{1,257},{2,258},{3,259},{4,260},{5,261},{6,262},{7,263},{8... | collective-permute-start | bytes 49160 | tf_op jit(solution)/shard_map/ppermute | solution.py:75
  67.8 6.2 %collective-permute-start.9 = (bf16[64,128]{1,0:T(8,128)(2,1)S(1)}, bf16[64,128]{1,0:T(8,128)(2,1)S(1)}, u32[]{:S(2)}, u32[]{:S(2)}) collective-permute-start(bf16[64,128]{1,0:T(8,128)(2,1)S(1)} %get-tuple-element.30), channel_id=1, source_target_pairs={{0,511},{1,508},{2,509},{3,510},{4,3},{5,0},{6,1},{7,2},{8,7},{9,4... | collective-permute-start | bytes 49160 | tf_op jit(solution)/shard_map/ppermute | solution.py:75
  74.1 5.5 %collective-permute-start.8 = (bf16[64,128]{1,0:T(8,128)(2,1)S(1)}, bf16[64,128]{1,0:T(8,128)(2,1)S(1)}, u32[]{:S(2)}, u32[]{:S(2)}) collective-permute-start(bf16[64,128]{1,0:T(8,128)(2,1)S(1)} %get-tuple-element.30), channel_id=1, source_target_pairs={{0,510},{1,511},{2,508},{3,509},{4,2},{5,3},{6,0},{7,1},{8,6},{9,7... | collective-permute-start | bytes 49160 | tf_op jit(solution)/shard_map/ppermute | solution.py:75
  89.2 4.6 %collective-permute-start.18 = (bf16[64,128]{1,0:T(8,128)(2,1)S(1)}, bf16[64,128]{1,0:T(8,128)(2,1)S(1)}, u32[]{:S(2)}, u32[]{:S(2)}) collective-permute-start(bf16[64,128]{1,0:T(8,128)(2,1)S(1)} %get-tuple-element.25), channel_id=1, source_target_pairs={{0,7},{1,4},{2,5},{3,6},{4,11},{5,8},{6,9},{7,10},{8,15},{9,12},{1... | collective-permute-start | bytes 49160 | tf_op jit(solution)/shard_map/ppermute | solution.py:75
  100.3 7.2 %collective-permute-start.26 = (bf16[64,128]{1,0:T(8,128)(2,1)S(1)}, bf16[64,128]{1,0:T(8,128)(2,1)S(1)}, u32[]{:S(2)}, u32[]{:S(2)}) collective-permute-start(bf16[64,128]{1,0:T(8,128)(2,1)S(1)} %get-tuple-element.26), channel_id=1, source_target_pairs={{0,259},{1,256},{2,257},{3,258},{4,263},{5,260},{6,261},{7,262},{8... | collective-permute-start | bytes 49160 | tf_op jit(solution)/shard_map/ppermute | solution.py:75
  107.6 5.0 %collective-permute-start.25 = (bf16[64,128]{1,0:T(8,128)(2,1)S(1)}, bf16[64,128]{1,0:T(8,128)(2,1)S(1)}, u32[]{:S(2)}, u32[]{:S(2)}) collective-permute-start(bf16[64,128]{1,0:T(8,128)(2,1)S(1)} %get-tuple-element.26), channel_id=1, source_target_pairs={{0,258},{1,259},{2,256},{3,257},{4,262},{5,263},{6,260},{7,261},{8... | collective-permute-start | bytes 49160 | tf_op jit(solution)/shard_map/ppermute | solution.py:75
  112.6 5.1 %collective-permute-start.24 = (bf16[64,128]{1,0:T(8,128)(2,1)S(1)}, bf16[64,128]{1,0:T(8,128)(2,1)S(1)}, u32[]{:S(2)}, u32[]{:S(2)}) collective-permute-start(bf16[64,128]{1,0:T(8,128)(2,1)S(1)} %get-tuple-element.26), channel_id=1, source_target_pairs={{0,257},{1,258},{2,259},{3,256},{4,261},{5,262},{6,263},{7,260},{8... | collective-permute-start | bytes 49160 | tf_op jit(solution)/shard_map/ppermute | solution.py:75
  120.8 5.8 %collective-permute-start.22 = (bf16[64,128]{1,0:T(8,128)(2,1)S(1)}, bf16[64,128]{1,0:T(8,128)(2,1)S(1)}, u32[]{:S(2)}, u32[]{:S(2)}) collective-permute-start(bf16[64,128]{1,0:T(8,128)(2,1)S(1)} %get-tuple-element.27), channel_id=1, source_target_pairs={{0,511},{1,508},{2,509},{3,510},{4,3},{5,0},{6,1},{7,2},{8,7},{9,4... | collective-permute-start | bytes 49160 | tf_op jit(solution)/shard_map/ppermute | solution.py:75
  126.6 7.1 %collective-permute-start.21 = (bf16[64,128]{1,0:T(8,128)(2,1)S(1)}, bf16[64,128]{1,0:T(8,128)(2,1)S(1)}, u32[]{:S(2)}, u32[]{:S(2)}) collective-permute-start(bf16[64,128]{1,0:T(8,128)(2,1)S(1)} %get-tuple-element.27), channel_id=1, source_target_pairs={{0,510},{1,511},{2,508},{3,509},{4,2},{5,3},{6,0},{7,1},{8,6},{9,7... | collective-permute-start | bytes 49160 | tf_op jit(solution)/shard_map/ppermute | solution.py:75
  133.7 3.1 %collective-permute-start.20 = (bf16[64,128]{1,0:T(8,128)(2,1)S(1)}, bf16[64,128]{1,0:T(8,128)(2,1)S(1)}, u32[]{:S(2)}, u32[]{:S(2)}) collective-permute-start(bf16[64,128]{1,0:T(8,128)(2,1)S(1)} %get-tuple-element.27), channel_id=1, source_target_pairs={{0,509},{1,510},{2,511},{3,508},{4,1},{5,2},{6,3},{7,0},{8,5},{9,6... | collective-permute-start | bytes 49160 | tf_op jit(solution)/shard_map/ppermute | solution.py:75
  143.2 4.7 %collective-permute-start.30 = (bf16[64,128]{1,0:T(8,128)(2,1)S(1)}, bf16[64,128]{1,0:T(8,128)(2,1)S(1)}, u32[]{:S(2)}, u32[]{:S(2)}) collective-permute-start(bf16[64,128]{1,0:T(8,128)(2,1)S(1)} %get-tuple-element.22), channel_id=1, source_target_pairs={{0,7},{1,4},{2,5},{3,6},{4,11},{5,8},{6,9},{7,10},{8,15},{9,12},{1... | collective-permute-start | bytes 49160 | tf_op jit(solution)/shard_map/ppermute | solution.py:75
  153.8 9.0 %collective-permute-start.38 = (bf16[64,128]{1,0:T(8,128)(2,1)S(1)}, bf16[64,128]{1,0:T(8,128)(2,1)S(1)}, u32[]{:S(2)}, u32[]{:S(2)}) collective-permute-start(bf16[64,128]{1,0:T(8,128)(2,1)S(1)} %get-tuple-element.23), channel_id=1, source_target_pairs={{0,259},{1,256},{2,257},{3,258},{4,263},{5,260},{6,261},{7,262},{8... | collective-permute-start | bytes 49160 | tf_op jit(solution)/shard_map/ppermute | solution.py:75
  165.7 6.0 %collective-permute-start.36 = (bf16[64,128]{1,0:T(8,128)(2,1)S(1)}, bf16[64,128]{1,0:T(8,128)(2,1)S(1)}, u32[]{:S(2)}, u32[]{:S(2)}) collective-permute-start(bf16[64,128]{1,0:T(8,128)(2,1)S(1)} %get-tuple-element.23), channel_id=1, source_target_pairs={{0,257},{1,258},{2,259},{3,256},{4,261},{5,262},{6,263},{7,260},{8... | collective-permute-start | bytes 49160 | tf_op jit(solution)/shard_map/ppermute | solution.py:75
  174.2 6.3 %collective-permute-start.34 = (bf16[64,128]{1,0:T(8,128)(2,1)S(1)}, bf16[64,128]{1,0:T(8,128)(2,1)S(1)}, u32[]{:S(2)}, u32[]{:S(2)}) collective-permute-start(bf16[64,128]{1,0:T(8,128)(2,1)S(1)} %get-tuple-element.24), channel_id=1, source_target_pairs={{0,511},{1,508},{2,509},{3,510},{4,3},{5,0},{6,1},{7,2},{8,7},{9,4... | collective-permute-start | bytes 49160 | tf_op jit(solution)/shard_map/ppermute | solution.py:75
  180.6 7.9 %collective-permute-start.33 = (bf16[64,128]{1,0:T(8,128)(2,1)S(1)}, bf16[64,128]{1,0:T(8,128)(2,1)S(1)}, u32[]{:S(2)}, u32[]{:S(2)}) collective-permute-start(bf16[64,128]{1,0:T(8,128)(2,1)S(1)} %get-tuple-element.24), channel_id=1, source_target_pairs={{0,510},{1,511},{2,508},{3,509},{4,2},{5,3},{6,0},{7,1},{8,6},{9,7... | collective-permute-start | bytes 49160 | tf_op jit(solution)/shard_map/ppermute | solution.py:75
  197.9 4.6 %collective-permute-start.42 = (bf16[64,128]{1,0:T(8,128)(2,1)S(1)}, bf16[64,128]{1,0:T(8,128)(2,1)S(1)}, u32[]{:S(2)}, u32[]{:S(2)}) collective-permute-start(bf16[64,128]{1,0:T(8,128)(2,1)S(1)} %get-tuple-element.19), channel_id=1, source_target_pairs={{0,7},{1,4},{2,5},{3,6},{4,11},{5,8},{6,9},{7,10},{8,15},{9,12},{1... | collective-permute-start | bytes 49160 | tf_op jit(solution)/shard_map/ppermute | solution.py:75
  208.5 8.0 %collective-permute-start.50 = (bf16[64,128]{1,0:T(8,128)(2,1)S(1)}, bf16[64,128]{1,0:T(8,128)(2,1)S(1)}, u32[]{:S(2)}, u32[]{:S(2)}) collective-permute-start(bf16[64,128]{1,0:T(8,128)(2,1)S(1)} %get-tuple-element.20), channel_id=1, source_target_pairs={{0,259},{1,256},{2,257},{3,258},{4,263},{5,260},{6,261},{7,262},{8... | collective-permute-start | bytes 49160 | tf_op jit(solution)/shard_map/ppermute | solution.py:75
  219.5 6.9 %collective-permute-start.48 = (bf16[64,128]{1,0:T(8,128)(2,1)S(1)}, bf16[64,128]{1,0:T(8,128)(2,1)S(1)}, u32[]{:S(2)}, u32[]{:S(2)}) collective-permute-start(bf16[64,128]{1,0:T(8,128)(2,1)S(1)} %get-tuple-element.20), channel_id=1, source_target_pairs={{0,257},{1,258},{2,259},{3,256},{4,261},{5,262},{6,263},{7,260},{8... | collective-permute-start | bytes 49160 | tf_op jit(solution)/shard_map/ppermute | solution.py:75
  229.0 6.3 %collective-permute-start.46 = (bf16[64,128]{1,0:T(8,128)(2,1)S(1)}, bf16[64,128]{1,0:T(8,128)(2,1)S(1)}, u32[]{:S(2)}, u32[]{:S(2)}) collective-permute-start(bf16[64,128]{1,0:T(8,128)(2,1)S(1)} %get-tuple-element.21), channel_id=1, source_target_pairs={{0,511},{1,508},{2,509},{3,510},{4,3},{5,0},{6,1},{7,2},{8,7},{9,4... | collective-permute-start | bytes 49160 | tf_op jit(solution)/shard_map/ppermute | solution.py:75
  235.3 7.1 %collective-permute-start.45 = (bf16[64,128]{1,0:T(8,128)(2,1)S(1)}, bf16[64,128]{1,0:T(8,128)(2,1)S(1)}, u32[]{:S(2)}, u32[]{:S(2)}) collective-permute-start(bf16[64,128]{1,0:T(8,128)(2,1)S(1)} %get-tuple-element.21), channel_id=1, source_target_pairs={{0,510},{1,511},{2,508},{3,509},{4,2},{5,3},{6,0},{7,1},{8,6},{9,7... | collective-permute-start | bytes 49160 | tf_op jit(solution)/shard_map/ppermute | solution.py:75
  242.5 3.1 %collective-permute-start.44 = (bf16[64,128]{1,0:T(8,128)(2,1)S(1)}, bf16[64,128]{1,0:T(8,128)(2,1)S(1)}, u32[]{:S(2)}, u32[]{:S(2)}) collective-permute-start(bf16[64,128]{1,0:T(8,128)(2,1)S(1)} %get-tuple-element.21), channel_id=1, source_target_pairs={{0,509},{1,510},{2,511},{3,508},{4,1},{5,2},{6,3},{7,0},{8,5},{9,6... | collective-permute-start | bytes 49160 | tf_op jit(solution)/shard_map/ppermute | solution.py:75
  245.7 3.1 %collective-permute-start.43 = (bf16[64,128]{1,0:T(8,128)(2,1)S(1)}, bf16[64,128]{1,0:T(8,128)(2,1)S(1)}, u32[]{:S(2)}, u32[]{:S(2)}) collective-permute-start(bf16[64,128]{1,0:T(8,128)(2,1)S(1)} %get-tuple-element.21), channel_id=1, source_target_pairs={{0,508},{1,509},{2,510},{3,511},{4,0},{5,1},{6,2},{7,3},{8,4},{9,5... | collective-permute-start | bytes 49160 | tf_op jit(solution)/shard_map/ppermute | solution.py:75
  253.9 4.3 %collective-permute-start.51 = (bf16[3,4,64,128]{3,2,1,0:T(8,128)(2,1)S(1)}, bf16[3,4,64,128]{3,2,1,0:T(8,128)(2,1)S(1)}, u32[]{:S(2)}, u32[]{:S(2)}) collective-permute-start(bf16[3,4,64,128]{3,2,1,0:T(8,128)(2,1)S(1)} %broadcast_select_fusion), channel_id=1, source_target_pairs={{0,1},{1,2},{2,3},{3,0},{4,5},{5,6},{6,7},{7,4},{8,9},{9,10},{10,1... | collective-permute-start | bytes 589832 | tf_op jit(solution)/shard_map/ppermute | solution.py:23
  266.1 5.1 %collective-permute-done.52 = bf16[3,4,64,128]{3,2,1,0:T(8,128)(2,1)S(1)} collective-permute-done((bf16[3,4,64,128]{3,2,1,0:T(8,128)(2,1)S(1)}, bf16[3,4,64,128]{3,2,1,0:T(8,128)(2,1)S(1)}, u32[]{:S(2)}, u32[]{:S(2)}) %collective-permute-start.52) | collective-permute-done | bytes 196640 | tf_op jit(solution)/shard_map/ppermute | solution.py:23
  (144 shorter events, 84.9 us)
Async XLA Ops:
  2.0 25.9 %collective-permute-start = (s32[]{:T(128)}, s32[]{:T(128)}, u32[]{:S(2)}, u32[]{:S(2)}) collective-permute-start(s32[]{:T(128)} %bitcast.2), channel_id=1, source_target_pairs={{0,508},{4,0},{8,4},{12,8},{16,12},{20,16},{24,20},{28,24},{32,28}... | collective-permute-start | bytes 20 | tf_op jit(solution)/shard_map/ppermute | solution.py:55
  21.5 65.7 %all-to-all-start = ((bf16[3,128,4,128]{3,1,0,2:T(8,128)(2,1)}), bf16[3,128,4,128]{3,1,0,2:T(8,128)(2,1)S(1)}, u32[]{:S(2)}, u32[]{:S(2)}) async-start(bf16[3,128,4,128]{3,1,0,2:T(8,128)(2,1)} %copy.74), calls=%async_computation | async-start | bytes 786432 | tf_op jit(solution)/shard_map/all_to_all | solution.py:57
  38.8 21.2 %collective-permute-start.3 = (bf16[64,128]{1,0:T(8,128)(2,1)S(1)}, bf16[64,128]{1,0:T(8,128)(2,1)S(1)}, u32[]{:S(2)}, u32[]{:S(2)}) collective-permute-start(bf16[64,128]{1,0:T(8,128)(2,1)S(1)} %get-tuple-element.28), channel_id=1, source_target_pairs={{0,6},{1,7},{2,4},{3,5},{4,10},{5,11},{6,8},{7,9},{8,14},{9,15},{1... | collective-permute-start | bytes 49160 | tf_op jit(solution)/shard_map/ppermute | solution.py:75
  42.1 19.9 %collective-permute-start.2 = (bf16[64,128]{1,0:T(8,128)(2,1)S(1)}, bf16[64,128]{1,0:T(8,128)(2,1)S(1)}, u32[]{:S(2)}, u32[]{:S(2)}) collective-permute-start(bf16[64,128]{1,0:T(8,128)(2,1)S(1)} %get-tuple-element.28), channel_id=1, source_target_pairs={{0,5},{1,6},{2,7},{3,4},{4,9},{5,10},{6,11},{7,8},{8,13},{9,14},{1... | collective-permute-start | bytes 49160 | tf_op jit(solution)/shard_map/ppermute | solution.py:75
  45.1 22.7 %collective-permute-start.1 = (bf16[64,128]{1,0:T(8,128)(2,1)S(1)}, bf16[64,128]{1,0:T(8,128)(2,1)S(1)}, u32[]{:S(2)}, u32[]{:S(2)}) collective-permute-start(bf16[64,128]{1,0:T(8,128)(2,1)S(1)} %get-tuple-element.28), channel_id=1, source_target_pairs={{0,4},{1,5},{2,6},{3,7},{4,8},{5,9},{6,10},{7,11},{8,12},{9,13},{1... | collective-permute-start | bytes 49160 | tf_op jit(solution)/shard_map/ppermute | solution.py:75
  48.1 25.9 %collective-permute-start.14 = (bf16[64,128]{1,0:T(8,128)(2,1)S(1)}, bf16[64,128]{1,0:T(8,128)(2,1)S(1)}, u32[]{:S(2)}, u32[]{:S(2)}) collective-permute-start(bf16[64,128]{1,0:T(8,128)(2,1)S(1)} %get-tuple-element.29), channel_id=1, source_target_pairs={{0,259},{1,256},{2,257},{3,258},{4,263},{5,260},{6,261},{7,262},{8... | collective-permute-start | bytes 49160 | tf_op jit(solution)/shard_map/ppermute | solution.py:75
  51.6 28.0 %collective-permute-start.13 = (bf16[64,128]{1,0:T(8,128)(2,1)S(1)}, bf16[64,128]{1,0:T(8,128)(2,1)S(1)}, u32[]{:S(2)}, u32[]{:S(2)}) collective-permute-start(bf16[64,128]{1,0:T(8,128)(2,1)S(1)} %get-tuple-element.29), channel_id=1, source_target_pairs={{0,258},{1,259},{2,256},{3,257},{4,262},{5,263},{6,260},{7,261},{8... | collective-permute-start | bytes 49160 | tf_op jit(solution)/shard_map/ppermute | solution.py:75
  60.1 22.1 %collective-permute-start.12 = (bf16[64,128]{1,0:T(8,128)(2,1)S(1)}, bf16[64,128]{1,0:T(8,128)(2,1)S(1)}, u32[]{:S(2)}, u32[]{:S(2)}) collective-permute-start(bf16[64,128]{1,0:T(8,128)(2,1)S(1)} %get-tuple-element.29), channel_id=1, source_target_pairs={{0,257},{1,258},{2,259},{3,256},{4,261},{5,262},{6,263},{7,260},{8... | collective-permute-start | bytes 49160 | tf_op jit(solution)/shard_map/ppermute | solution.py:75
  62.0 22.8 %collective-permute-start.11 = (bf16[64,128]{1,0:T(8,128)(2,1)S(1)}, bf16[64,128]{1,0:T(8,128)(2,1)S(1)}, u32[]{:S(2)}, u32[]{:S(2)}) collective-permute-start(bf16[64,128]{1,0:T(8,128)(2,1)S(1)} %get-tuple-element.29), channel_id=1, source_target_pairs={{0,256},{1,257},{2,258},{3,259},{4,260},{5,261},{6,262},{7,263},{8... | collective-permute-start | bytes 49160 | tf_op jit(solution)/shard_map/ppermute | solution.py:75
  93.9 18.7 %collective-permute-start.17 = (bf16[64,128]{1,0:T(8,128)(2,1)S(1)}, bf16[64,128]{1,0:T(8,128)(2,1)S(1)}, u32[]{:S(2)}, u32[]{:S(2)}) collective-permute-start(bf16[64,128]{1,0:T(8,128)(2,1)S(1)} %get-tuple-element.25), channel_id=1, source_target_pairs={{0,6},{1,7},{2,4},{3,5},{4,10},{5,11},{6,8},{7,9},{8,14},{9,15},{1... | collective-permute-start | bytes 49160 | tf_op jit(solution)/shard_map/ppermute | solution.py:75
  95.8 21.9 %collective-permute-start.16 = (bf16[64,128]{1,0:T(8,128)(2,1)S(1)}, bf16[64,128]{1,0:T(8,128)(2,1)S(1)}, u32[]{:S(2)}, u32[]{:S(2)}) collective-permute-start(bf16[64,128]{1,0:T(8,128)(2,1)S(1)} %get-tuple-element.25), channel_id=1, source_target_pairs={{0,5},{1,6},{2,7},{3,4},{4,9},{5,10},{6,11},{7,8},{8,13},{9,14},{1... | collective-permute-start | bytes 49160 | tf_op jit(solution)/shard_map/ppermute | solution.py:75
  97.8 23.0 %collective-permute-start.15 = (bf16[64,128]{1,0:T(8,128)(2,1)S(1)}, bf16[64,128]{1,0:T(8,128)(2,1)S(1)}, u32[]{:S(2)}, u32[]{:S(2)}) collective-permute-start(bf16[64,128]{1,0:T(8,128)(2,1)S(1)} %get-tuple-element.25), channel_id=1, source_target_pairs={{0,4},{1,5},{2,6},{3,7},{4,8},{5,9},{6,10},{7,11},{8,12},{9,13},{1... | collective-permute-start | bytes 49160 | tf_op jit(solution)/shard_map/ppermute | solution.py:75
  100.3 26.2 %collective-permute-start.26 = (bf16[64,128]{1,0:T(8,128)(2,1)S(1)}, bf16[64,128]{1,0:T(8,128)(2,1)S(1)}, u32[]{:S(2)}, u32[]{:S(2)}) collective-permute-start(bf16[64,128]{1,0:T(8,128)(2,1)S(1)} %get-tuple-element.26), channel_id=1, source_target_pairs={{0,259},{1,256},{2,257},{3,258},{4,263},{5,260},{6,261},{7,262},{8... | collective-permute-start | bytes 49160 | tf_op jit(solution)/shard_map/ppermute | solution.py:75
  107.6 26.2 %collective-permute-start.25 = (bf16[64,128]{1,0:T(8,128)(2,1)S(1)}, bf16[64,128]{1,0:T(8,128)(2,1)S(1)}, u32[]{:S(2)}, u32[]{:S(2)}) collective-permute-start(bf16[64,128]{1,0:T(8,128)(2,1)S(1)} %get-tuple-element.26), channel_id=1, source_target_pairs={{0,258},{1,259},{2,256},{3,257},{4,262},{5,263},{6,260},{7,261},{8... | collective-permute-start | bytes 49160 | tf_op jit(solution)/shard_map/ppermute | solution.py:75
  112.6 24.3 %collective-permute-start.24 = (bf16[64,128]{1,0:T(8,128)(2,1)S(1)}, bf16[64,128]{1,0:T(8,128)(2,1)S(1)}, u32[]{:S(2)}, u32[]{:S(2)}) collective-permute-start(bf16[64,128]{1,0:T(8,128)(2,1)S(1)} %get-tuple-element.26), channel_id=1, source_target_pairs={{0,257},{1,258},{2,259},{3,256},{4,261},{5,262},{6,263},{7,260},{8... | collective-permute-start | bytes 49160 | tf_op jit(solution)/shard_map/ppermute | solution.py:75
  117.7 22.3 %collective-permute-start.23 = (bf16[64,128]{1,0:T(8,128)(2,1)S(1)}, bf16[64,128]{1,0:T(8,128)(2,1)S(1)}, u32[]{:S(2)}, u32[]{:S(2)}) collective-permute-start(bf16[64,128]{1,0:T(8,128)(2,1)S(1)} %get-tuple-element.26), channel_id=1, source_target_pairs={{0,256},{1,257},{2,258},{3,259},{4,260},{5,261},{6,262},{7,263},{8... | collective-permute-start | bytes 49160 | tf_op jit(solution)/shard_map/ppermute | solution.py:75
  120.8 19.2 %collective-permute-start.22 = (bf16[64,128]{1,0:T(8,128)(2,1)S(1)}, bf16[64,128]{1,0:T(8,128)(2,1)S(1)}, u32[]{:S(2)}, u32[]{:S(2)}) collective-permute-start(bf16[64,128]{1,0:T(8,128)(2,1)S(1)} %get-tuple-element.27), channel_id=1, source_target_pairs={{0,511},{1,508},{2,509},{3,510},{4,3},{5,0},{6,1},{7,2},{8,7},{9,4... | collective-permute-start | bytes 49160 | tf_op jit(solution)/shard_map/ppermute | solution.py:75
  143.2 19.5 %collective-permute-start.30 = (bf16[64,128]{1,0:T(8,128)(2,1)S(1)}, bf16[64,128]{1,0:T(8,128)(2,1)S(1)}, u32[]{:S(2)}, u32[]{:S(2)}) collective-permute-start(bf16[64,128]{1,0:T(8,128)(2,1)S(1)} %get-tuple-element.22), channel_id=1, source_target_pairs={{0,7},{1,4},{2,5},{3,6},{4,11},{5,8},{6,9},{7,10},{8,15},{9,12},{1... | collective-permute-start | bytes 49160 | tf_op jit(solution)/shard_map/ppermute | solution.py:75
  149.9 21.8 %collective-permute-start.28 = (bf16[64,128]{1,0:T(8,128)(2,1)S(1)}, bf16[64,128]{1,0:T(8,128)(2,1)S(1)}, u32[]{:S(2)}, u32[]{:S(2)}) collective-permute-start(bf16[64,128]{1,0:T(8,128)(2,1)S(1)} %get-tuple-element.22), channel_id=1, source_target_pairs={{0,5},{1,6},{2,7},{3,4},{4,9},{5,10},{6,11},{7,8},{8,13},{9,14},{1... | collective-permute-start | bytes 49160 | tf_op jit(solution)/shard_map/ppermute | solution.py:75
  151.9 22.4 %collective-permute-start.27 = (bf16[64,128]{1,0:T(8,128)(2,1)S(1)}, bf16[64,128]{1,0:T(8,128)(2,1)S(1)}, u32[]{:S(2)}, u32[]{:S(2)}) collective-permute-start(bf16[64,128]{1,0:T(8,128)(2,1)S(1)} %get-tuple-element.22), channel_id=1, source_target_pairs={{0,4},{1,5},{2,6},{3,7},{4,8},{5,9},{6,10},{7,11},{8,12},{9,13},{1... | collective-permute-start | bytes 49160 | tf_op jit(solution)/shard_map/ppermute | solution.py:75
  153.8 26.8 %collective-permute-start.38 = (bf16[64,128]{1,0:T(8,128)(2,1)S(1)}, bf16[64,128]{1,0:T(8,128)(2,1)S(1)}, u32[]{:S(2)}, u32[]{:S(2)}) collective-permute-start(bf16[64,128]{1,0:T(8,128)(2,1)S(1)} %get-tuple-element.23), channel_id=1, source_target_pairs={{0,259},{1,256},{2,257},{3,258},{4,263},{5,260},{6,261},{7,262},{8... | collective-permute-start | bytes 49160 | tf_op jit(solution)/shard_map/ppermute | solution.py:75
  162.8 25.7 %collective-permute-start.37 = (bf16[64,128]{1,0:T(8,128)(2,1)S(1)}, bf16[64,128]{1,0:T(8,128)(2,1)S(1)}, u32[]{:S(2)}, u32[]{:S(2)}) collective-permute-start(bf16[64,128]{1,0:T(8,128)(2,1)S(1)} %get-tuple-element.23), channel_id=1, source_target_pairs={{0,258},{1,259},{2,256},{3,257},{4,262},{5,263},{6,260},{7,261},{8... | collective-permute-start | bytes 49160 | tf_op jit(solution)/shard_map/ppermute | solution.py:75
  165.7 25.8 %collective-permute-start.36 = (bf16[64,128]{1,0:T(8,128)(2,1)S(1)}, bf16[64,128]{1,0:T(8,128)(2,1)S(1)}, u32[]{:S(2)}, u32[]{:S(2)}) collective-permute-start(bf16[64,128]{1,0:T(8,128)(2,1)S(1)} %get-tuple-element.23), channel_id=1, source_target_pairs={{0,257},{1,258},{2,259},{3,256},{4,261},{5,262},{6,263},{7,260},{8... | collective-permute-start | bytes 49160 | tf_op jit(solution)/shard_map/ppermute | solution.py:75
  171.7 22.4 %collective-permute-start.35 = (bf16[64,128]{1,0:T(8,128)(2,1)S(1)}, bf16[64,128]{1,0:T(8,128)(2,1)S(1)}, u32[]{:S(2)}, u32[]{:S(2)}) collective-permute-start(bf16[64,128]{1,0:T(8,128)(2,1)S(1)} %get-tuple-element.23), channel_id=1, source_target_pairs={{0,256},{1,257},{2,258},{3,259},{4,260},{5,261},{6,262},{7,263},{8... | collective-permute-start | bytes 49160 | tf_op jit(solution)/shard_map/ppermute | solution.py:75
  174.2 19.9 %collective-permute-start.34 = (bf16[64,128]{1,0:T(8,128)(2,1)S(1)}, bf16[64,128]{1,0:T(8,128)(2,1)S(1)}, u32[]{:S(2)}, u32[]{:S(2)}) collective-permute-start(bf16[64,128]{1,0:T(8,128)(2,1)S(1)} %get-tuple-element.24), channel_id=1, source_target_pairs={{0,511},{1,508},{2,509},{3,510},{4,3},{5,0},{6,1},{7,2},{8,7},{9,4... | collective-permute-start | bytes 49160 | tf_op jit(solution)/shard_map/ppermute | solution.py:75
  204.5 22.0 %collective-permute-start.40 = (bf16[64,128]{1,0:T(8,128)(2,1)S(1)}, bf16[64,128]{1,0:T(8,128)(2,1)S(1)}, u32[]{:S(2)}, u32[]{:S(2)}) collective-permute-start(bf16[64,128]{1,0:T(8,128)(2,1)S(1)} %get-tuple-element.19), channel_id=1, source_target_pairs={{0,5},{1,6},{2,7},{3,4},{4,9},{5,10},{6,11},{7,8},{8,13},{9,14},{1... | collective-permute-start | bytes 49160 | tf_op jit(solution)/shard_map/ppermute | solution.py:75
  206.4 22.6 %collective-permute-start.39 = (bf16[64,128]{1,0:T(8,128)(2,1)S(1)}, bf16[64,128]{1,0:T(8,128)(2,1)S(1)}, u32[]{:S(2)}, u32[]{:S(2)}) collective-permute-start(bf16[64,128]{1,0:T(8,128)(2,1)S(1)} %get-tuple-element.19), channel_id=1, source_target_pairs={{0,4},{1,5},{2,6},{3,7},{4,8},{5,9},{6,10},{7,11},{8,12},{9,13},{1... | collective-permute-start | bytes 49160 | tf_op jit(solution)/shard_map/ppermute | solution.py:75
  208.5 26.9 %collective-permute-start.50 = (bf16[64,128]{1,0:T(8,128)(2,1)S(1)}, bf16[64,128]{1,0:T(8,128)(2,1)S(1)}, u32[]{:S(2)}, u32[]{:S(2)}) collective-permute-start(bf16[64,128]{1,0:T(8,128)(2,1)S(1)} %get-tuple-element.20), channel_id=1, source_target_pairs={{0,259},{1,256},{2,257},{3,258},{4,263},{5,260},{6,261},{7,262},{8... | collective-permute-start | bytes 49160 | tf_op jit(solution)/shard_map/ppermute | solution.py:75
  216.5 26.0 %collective-permute-start.49 = (bf16[64,128]{1,0:T(8,128)(2,1)S(1)}, bf16[64,128]{1,0:T(8,128)(2,1)S(1)}, u32[]{:S(2)}, u32[]{:S(2)}) collective-permute-start(bf16[64,128]{1,0:T(8,128)(2,1)S(1)} %get-tuple-element.20), channel_id=1, source_target_pairs={{0,258},{1,259},{2,256},{3,257},{4,262},{5,263},{6,260},{7,261},{8... | collective-permute-start | bytes 49160 | tf_op jit(solution)/shard_map/ppermute | solution.py:75
  219.5 26.2 %collective-permute-start.48 = (bf16[64,128]{1,0:T(8,128)(2,1)S(1)}, bf16[64,128]{1,0:T(8,128)(2,1)S(1)}, u32[]{:S(2)}, u32[]{:S(2)}) collective-permute-start(bf16[64,128]{1,0:T(8,128)(2,1)S(1)} %get-tuple-element.20), channel_id=1, source_target_pairs={{0,257},{1,258},{2,259},{3,256},{4,261},{5,262},{6,263},{7,260},{8... | collective-permute-start | bytes 49160 | tf_op jit(solution)/shard_map/ppermute | solution.py:75
  226.5 22.3 %collective-permute-start.47 = (bf16[64,128]{1,0:T(8,128)(2,1)S(1)}, bf16[64,128]{1,0:T(8,128)(2,1)S(1)}, u32[]{:S(2)}, u32[]{:S(2)}) collective-permute-start(bf16[64,128]{1,0:T(8,128)(2,1)S(1)} %get-tuple-element.20), channel_id=1, source_target_pairs={{0,256},{1,257},{2,258},{3,259},{4,260},{5,261},{6,262},{7,263},{8... | collective-permute-start | bytes 49160 | tf_op jit(solution)/shard_map/ppermute | solution.py:75
  229.0 19.8 %collective-permute-start.46 = (bf16[64,128]{1,0:T(8,128)(2,1)S(1)}, bf16[64,128]{1,0:T(8,128)(2,1)S(1)}, u32[]{:S(2)}, u32[]{:S(2)}) collective-permute-start(bf16[64,128]{1,0:T(8,128)(2,1)S(1)} %get-tuple-element.21), channel_id=1, source_target_pairs={{0,511},{1,508},{2,509},{3,510},{4,3},{5,0},{6,1},{7,2},{8,7},{9,4... | collective-permute-start | bytes 49160 | tf_op jit(solution)/shard_map/ppermute | solution.py:75
  (27 other events, 272.5 us)
